TPU v7x, 32 devices: a whole 2x2x4 slice. The times are simulated.
32 devices in a mesh: grp: 2 (over y), gx: 16 (over z, x, core).
Axes of the slice: x: 2, y: 2, z: 4, core: 2. Of those that a mesh axis runs over, the one named last changes fastest.
Arguments:
- volume: float32 [512, 896], P(('grp', 'gx')), parts along dimension 0, may hold values from -45 to 45
- bank: float32 [8, 4096], P(None, 'gx'), may hold values from -43 to 43
- orient: int32 [8], replicated, may hold values from 0 to 47
- bank_id: int32 [8], replicated, may hold values from 0 to 7, each once
- counts: int32 [8], replicated, may hold values from 1 to 16
Outputs:
- fields: float32 [4, 512, 896], P(None, ('grp', 'gx')), parts along dimension 1
There are 2 independent parts, one for each index of `grp`. A program takes and returns all parts, laid end to end along the dimension named above; an argument that names none is the same for every part. Nothing has to cross between parts.
Inputs may be any that keep to these rules, and one draw needn't show every extreme that they name: `bank_id`: each of the 8 base templates is named by exactly one list entry.
All inputs are finite; a program needn't handle non-finite values.
Results may differ from a plain program's by a relative error of at most 0.0003.
Values sent between devices are 32-bit elements; how exact they have to be, the bound alone decides.
No kernel may reach another device: no remote copies, remote signals or barrier semaphores. Data moves between devices by JAX's collectives and lax.ppermute only.
A program may use at most 64 MiB of HBM per device.

v0:
```python
import math
import jax
import jax.numpy as jnp
import numpy as np
from jax import lax
from jax.sharding import PartitionSpec as P

BY = 8
BZ = 112
TS = 16
NT = 8
FIELDS = 4
epsilon = 1e-05
sharpness = 80.0
AXIS_ORDERS = np.array([[0, 1, 2], [0, 2, 1], [1, 0, 2], [1, 2, 0], [2, 0, 1], [2, 1, 0]], np.int32)


def extended(x, sides, width):
    for axis, dim in sides:
        size, length = (lax.axis_size(axis), x.shape[dim])
        up = [(i, (i + 1) % size) for i in range(size - 1)]
        down = [(j, i) for i, j in up]
        last = lax.slice_in_dim(x, length - width, length, axis=dim)
        leading = lax.slice_in_dim(x, 0, width, axis=dim)
        before = lax.ppermute(last, axis, up)
        after = lax.ppermute(leading, axis, down)
        x = jnp.concatenate([before, x, after], axis=dim)
    return x


def padded_length(length):
    return -(-length // 128) * 128


def rotate_template(flat_base, orient_one):
    coords = jnp.arange(TS**3, dtype=jnp.int32)
    index_set = jnp.stack([coords // (TS * TS), coords // TS % TS, coords % TS])
    order_row = orient_one // 8
    flip_set = orient_one % 8
    picked = (jnp.arange(6, dtype=jnp.int32) == order_row).astype(jnp.int32)
    ordering = jnp.sum(picked[:, None] * jnp.asarray(AXIS_ORDERS), axis=0)
    source = jnp.zeros_like(coords)
    for axis_num in range(3):
        select = (ordering[axis_num] == jnp.arange(3, dtype=jnp.int32)).astype(jnp.int32)
        chosen = jnp.sum(select[:, None] * index_set, axis=0)
        flipped = flip_set // 2**axis_num % 2
        placed = chosen + flipped * (TS - 1 - 2 * chosen)
        source = source * TS + placed
    return flat_base[source]


def normalized_kernel(flat_base, orient_one):
    rotated = rotate_template(flat_base, orient_one)
    centered = rotated - jnp.mean(rotated)
    return centered / jnp.sqrt(jnp.sum(centered * centered) + epsilon)


def wave_tables(positions, targets, period, direction):
    turns = (positions[:, None] * targets[None, :] % period).astype(jnp.float32)
    phase = 2.0 * math.pi / period * turns
    return (jnp.cos(phase), direction * jnp.sin(phase))


def band_table(positions, targets, period):
    offset = (positions[:, None] - targets[None, :]) % period
    return (offset < TS).astype(jnp.float32)


def contract(letters, data, table):
    return jnp.einsum(letters, data, table, precision=lax.Precision.HIGHEST)


def spectrum_along(real_part, imag_part, cos_table, sin_table, letters):
    new_real = contract(letters, real_part, cos_table) - contract(letters, imag_part, sin_table)
    new_imag = contract(letters, real_part, sin_table) + contract(letters, imag_part, cos_table)
    return (new_real, new_imag)


def local(volume, bank, orient, bank_id, counts):
    rows_x = volume.shape[0]
    half = TS // 2
    grid = volume.reshape(rows_x, BY, BZ)
    len_x = rows_x + TS
    len_y = BY + TS
    len_z = padded_length(BZ + TS)
    gathered = lax.all_gather(bank, "gx", axis=1, tiled=True)
    kernels = jax.vmap(normalized_kernel)(gathered[bank_id], orient)
    field_in = extended(grid, (("gx", 0),), half)
    pos_x = jnp.arange(len_x, dtype=jnp.int32)
    out_x = jnp.arange(rows_x, dtype=jnp.int32)
    pos_y = half + jnp.arange(BY, dtype=jnp.int32)
    pos_z = half + jnp.arange(BZ, dtype=jnp.int32)
    freq_x = jnp.arange(len_x, dtype=jnp.int32)
    freq_y = jnp.arange(len_y, dtype=jnp.int32)
    freq_z = jnp.arange(len_z, dtype=jnp.int32)
    tmpl_pos = jnp.arange(TS, dtype=jnp.int32)
    cos_z, sin_z = wave_tables(pos_z, freq_z, len_z, -1.0)
    cos_y, sin_y = wave_tables(pos_y, freq_y, len_y, -1.0)
    cos_x, sin_x = wave_tables(pos_x, freq_x, len_x, -1.0)
    vol_re = contract("xyz,zk->xyk", field_in, cos_z)
    vol_im = contract("xyz,zk->xyk", field_in, sin_z)
    vol_re, vol_im = spectrum_along(vol_re, vol_im, cos_y, sin_y, "xyk,yj->xjk")
    vol_re, vol_im = spectrum_along(vol_re, vol_im, cos_x, sin_x, "xjk,xi->ijk")
    kcos_z, ksin_z = wave_tables(tmpl_pos, freq_z, len_z, -1.0)
    kcos_y, ksin_y = wave_tables(tmpl_pos, freq_y, len_y, -1.0)
    kcos_x, ksin_x = wave_tables(tmpl_pos, freq_x, len_x, -1.0)
    icos_y, isin_y = wave_tables(freq_y, jnp.arange(BY, dtype=jnp.int32), len_y, 1.0)
    icos_x, isin_x = wave_tables(freq_x, out_x, len_x, 1.0)
    icos_z, isin_z = wave_tables(freq_z, jnp.arange(BZ, dtype=jnp.int32), len_z, 1.0)
    inverse_scale = 1.0 / (len_x * len_y * len_z)

    def correlate(kernel_flat):
        kernel = kernel_flat.reshape(TS, TS, TS)
        kernel_re = contract("xyz,zk->xyk", kernel, kcos_z)
        kernel_im = contract("xyz,zk->xyk", kernel, ksin_z)
        kernel_re, kernel_im = spectrum_along(kernel_re, kernel_im, kcos_y, ksin_y, "xyk,yj->xjk")
        kernel_re, kernel_im = spectrum_along(kernel_re, kernel_im, kcos_x, ksin_x, "xjk,xi->ijk")
        prod_re = kernel_re * vol_re + kernel_im * vol_im
        prod_im = kernel_re * vol_im - kernel_im * vol_re
        prod_re, prod_im = spectrum_along(prod_re, prod_im, icos_y, isin_y, "ijk,jn->ink")
        prod_re, prod_im = spectrum_along(prod_re, prod_im, icos_x, isin_x, "ink,im->mnk")
        real_out = contract("mnk,kz->mnz", prod_re, icos_z) - contract(
            "mnk,kz->mnz", prod_im, isin_z
        )
        return real_out * inverse_scale

    numer = lax.map(correlate, kernels)
    squares = field_in * field_in
    energy = contract(
        "xyz,zn->xyn", squares, band_table(pos_z, jnp.arange(BZ, dtype=jnp.int32), len_z)
    )
    energy = contract(
        "xyn,ym->xmn", energy, band_table(pos_y, jnp.arange(BY, dtype=jnp.int32), len_y)
    )
    energy = contract("xmn,xl->lmn", energy, band_table(pos_x, out_x, len_x))
    scores = numer / jnp.sqrt(energy + epsilon)[None]
    weights = counts.astype(jnp.float32)
    weighted = weights[:, None, None, None] * jnp.exp(sharpness * scores)
    grouped = jnp.sum(weighted.reshape(FIELDS, NT // FIELDS, rows_x, BY, BZ), axis=1)
    totals = jnp.sum(weights.reshape(FIELDS, NT // FIELDS), axis=1)
    fields = jnp.log(grouped / totals[:, None, None, None])
    return fields.reshape(FIELDS, rows_x, BY * BZ)


def solution(mesh):
    in_specs = (P(("grp", "gx"), None), P(None, "gx"), P(), P(), P())
    out_specs = P(None, ("grp", "gx"), None)
    return jax.shard_map(local, mesh=mesh, in_specs=in_specs, out_specs=out_specs, check_vma=False)
```

profile of v0, /device:TPU:0, one launch (start us, length us, event | category | flops | bytes accessed | tf_op | source)
XLA Modules:
  0.0 316.0 jit_solution(17705312637097414959)
XLA Ops:
  0.0 0.8 fusion.433
  0.8 2.3 collective-permute-start
  3.3 1.3 collective-permute-start.1
  4.6 0.7 compare_select_fusion.3
  5.3 0.7 and_select_fusion.8
  6.1 0.8 multiply_reduce_fusion.4
  6.9 25.6 %all_gather.3 = f32[8,4096]{1,0:T(8,128)S(1)} all-gather(f32[8,256]{1,0:T(8,128)} %param.9), channel_id=1, replica_groups=mesh['grp'=2,'gx'=16] {'gx'}, dimensions={1}, use_global_device_ids=true | all-gather | bytes 139264 | tf_op jit(solution)/shard_map/all_gather | solution.py:86
  32.9 0.6 gather_fusion
  33.5 200.1 %gather_fusion.1 = f32[32768]{0:T(1024)S(1)} fusion(f32[8,4096]{1,0:T(8,128)S(1)} %gather_fusion, s32[32768]{0:T(1024)S(1)} %bitcast.250), kind=kCustom, calls=%fused_computation.1 | custom fusion | bytes 524288 | tf_op jit(solution)/shard_map/vmap()/gather | solution.py:49
  235.9 0.6 fusion.332
  236.6 0.6 fusion.336
  237.2 0.6 fusion.250
  239.8 0.6 fusion.249
  240.5 0.6 convolution_subtract_fusion.5
  241.0 0.6 convolution_add_fusion.4
  241.6 73.3 %while.12 = (s32[]{:T(128)}, f32[8,16,8,112]{3,2,1,0:T(8,128)S(1)}, f32[8,4096]{1,0:T(8,128)S(1)}, f32[32,24,128]{2,0,1:T(8,128)S(1)}, f32[32,24,128]{2,0,1:T(8,128)S(1)}, /*index=5*/s32[]{:T(128)}) while((s32[]{:T(128)}, f32[8,16,8,112]{3,2,1,0:T(8,128)S(1)}, f32[8,4096]{1,0:T(8,128)S(1)}, ...), condition=%wide.region_7.8_spmd.clone.clone, body=%wide.region_6.7_spmd.clone.clone.sunk | while | flops 234336256 | bytes 10379349 | solution.py:127
  245.4 0.6 fusion.548
  246.0 0.7 multiply_subtract_fusion.2
  254.6 0.6 fusion.548
  255.1 0.7 multiply_subtract_fusion.2
  263.7 0.6 fusion.548
  264.3 0.7 multiply_subtract_fusion.2
  272.8 0.6 fusion.548
  273.4 0.7 multiply_subtract_fusion.2
  282.0 0.6 fusion.548
  282.5 0.7 multiply_subtract_fusion.2
  291.1 0.6 fusion.548
  291.7 0.7 multiply_subtract_fusion.2
  300.2 0.6 fusion.548
  300.8 0.7 multiply_subtract_fusion.2
  310.0 0.7 multiply_subtract_fusion.2
  315.2 0.8 divide_log_fusion
  (208 shorter events, 67.2 us)
Async XLA Ops:
  0.8 233.9 %collective-permute-start = (f32[8,8,112]{2,1,0:T(8,128)S(1)}, f32[8,8,112]{2,1,0:T(8,128)S(1)}, u32[]{:S(2)}, u32[]{:S(2)}) collective-permute-start(f32[8,8,112]{2,1,0:T(8,128)S(1)} %slice.34), channel_id=1, source_target_pairs={{0,1},{1,2},{2,3},{3,4},{4,5},{5,6},{6,7},{7,8},{8,9},{9,10},{10,1... | collective-permute-start | bytes 86024 | tf_op jit(solution)/shard_map/ppermute | solution.py:25
  3.3 231.5 %collective-permute-start.1 = (f32[8,8,112]{2,1,0:T(8,128)S(1)}, f32[8,8,112]{2,1,0:T(8,128)S(1)}, u32[]{:S(2)}, u32[]{:S(2)}) collective-permute-start(f32[8,8,112]{2,1,0:T(8,128)S(1)} %slice.36), channel_id=1, source_target_pairs={{1,0},{2,1},{3,2},{4,3},{5,4},{6,5},{7,6},{8,7},{9,8},{10,9},{11,1... | collective-permute-start | bytes 86024 | tf_op jit(solution)/shard_map/ppermute | solution.py:26
  233.6 0.8 copy-start
  233.6 0.9 copy-start.1
where the time goes:
time: 316 us
  local copies, waits for them, and re-layouts  203 us (64%)
  matrix products  77.2 us (24%)
  blocking collectives  25.6 us (8%)
  other arithmetic  4.22 us (1%)
  starting transfers between devices  3.63 us (1%)
    gather x2, local copies, waits for them, and re-layouts, rotate_template(): return flat_base[source]  200 us
    dot_general x173, matrix products, contract(): return jnp.einsum(letters, data, table, precision=lax.Precision.HIGHEST)  77.2 us
    all_gather x1, blocking collectives, local(): gathered = lax.all_gather(bank, 'gx', axis=1, tiled=True)  25.6 us
  transfers between devices with their start and end apart: 2, of which 0 were waited for; matrix products, arithmetic and copies ran while one was open for 65% of the time, Pallas kernels for 0%

commit v1 on v0

--- a/solution.py
+++ b/solution.py
@@ -83,7 +83,22 @@
     len_x = rows_x + TS
     len_y = BY + TS
     len_z = padded_length(BZ + TS)
-    gathered = lax.all_gather(bank, "gx", axis=1, tiled=True)
+
+    def clear_the_plane(patch):
+        peer_axis = "gx"
+        left_arr, part_now = (jax.lax.axis_size(peer_axis), jax.lax.axis_index(peer_axis))
+        work_now, everything = (patch, 1)
+        while everything < left_arr:
+            val2 = jax.lax.ppermute(
+                work_now, peer_axis, [(dd, dd ^ everything) for dd in range(left_arr)]
+            )
+            met_up = jnp.concatenate([work_now, val2], axis=1)
+            a_next = jnp.concatenate([val2, work_now], axis=1)
+            work_now = jnp.where(part_now & everything == 0, met_up, a_next)
+            everything = 2 * everything
+        return work_now
+
+    gathered = clear_the_plane(bank)
     kernels = jax.vmap(normalized_kernel)(gathered[bank_id], orient)
     field_in = extended(grid, (("gx", 0),), half)
     pos_x = jnp.arange(len_x, dtype=jnp.int32)

time: 316 us -> 305 us (0.965)
  blocking collectives: 25.6 us -> 0 us
  starting transfers between devices: 3.63 us -> 14.2 us
  waiting for transfers between devices: 0.01 us -> 3.95 us
    all_gather x1 -> x0, blocking collectives: 25.6 us -> none  [local(): gathered = lax.all_gather(bank, 'gx', axis=1, tiled=True)]
    ppermute x0 -> x4, starting transfers between devices: none -> 10.9 us  [clear_the_plane(): jax.lax.ppermute(work_now, peer_axis, [(dd, dd ^ everything) for dd in ra...]
    ppermute x0 -> x4, waiting for transfers between devices: none -> 3.95 us  [clear_the_plane(): jax.lax.ppermute(work_now, peer_axis, [(dd, dd ^ everything) for dd in ra...]
  transfers between devices with their start and end apart: 2 -> 6, of which waited for: 0 -> 2; matrix products, arithmetic and copies ran while one was open for 65% -> 3% of each run, Pallas kernels for 0% -> 0%
where the time goes in v1:
time: 305 us
  local copies, waits for them, and re-layouts  204 us (67%)
  matrix products  77.2 us (25%)
  starting transfers between devices  14.2 us (5%)
  other arithmetic  4.26 us (1%)
  waiting for transfers between devices  3.95 us (1%)
    gather x2, local copies, waits for them, and re-layouts, rotate_template(): return flat_base[source]  200 us
    dot_general x173, matrix products, contract(): return jnp.einsum(letters, data, table, precision=lax.Precision.HIGHEST)  77.2 us
    ppermute x4, starting transfers between devices, clear_the_plane(): jax.lax.ppermute(work_now, peer_axis, [(dd, dd ^ everything) for dd in ra...  10.9 us
  transfers between devices with their start and end apart: 6, of which 2 were waited for; matrix products, arithmetic and copies ran while one was open for 3% of the time, Pallas kernels for 0%

profile of v1, /device:TPU:0, one launch (start us, length us, event | category | flops | bytes accessed | tf_op | source)
XLA Modules:
  0.0 305.0 jit_solution(11126233292213459844)
XLA Ops:
  0.5 0.8 fusion.433
  1.3 2.0 collective-permute-start.4
  3.3 1.3 collective-permute-start.5
  4.7 0.7 compare_select_fusion.3
  5.3 0.7 and_select_fusion.8
  6.1 0.8 multiply_reduce_fusion.4
  7.7 4.8 %collective-permute-start.1 = (f32[8,512]{1,0:T(8,128)S(1)}, f32[8,512]{1,0:T(8,128)S(1)}, u32[]{:S(2)}, u32[]{:S(2)}) collective-permute-start(f32[8,512]{1,0:T(8,128)S(1)} %maximum_select_fusion.3), channel_id=1, source_target_pairs={{0,2},{1,3},{2,0},{3,1},{4,6},{5,7},{6,4},{7,5},{8,10},{9,11},{10,... | collective-permute-start | bytes 49160 | tf_op jit(solution)/shard_map/ppermute | solution.py:92
  12.9 1.3 collective-permute-done.1
  14.3 3.0 collective-permute-start.2
  18.4 0.6 fusion.332
  19.1 0.6 fusion.336
  19.7 0.6 fusion.250
  21.8 0.6 fusion.249
  22.5 0.6 convolution_subtract_fusion.5
  23.0 0.6 convolution_add_fusion.4
  23.9 2.7 collective-permute-start.3
  26.8 2.6 collective-permute-done.3
  29.4 0.6 gather_fusion
  30.0 200.3 %gather_fusion.1 = f32[32768]{0:T(1024)S(1)} fusion(f32[8,4096]{1,0:T(8,128)S(1)} %gather_fusion, s32[32768]{0:T(1024)S(1)} %bitcast.250), kind=kCustom, calls=%fused_computation.1 | custom fusion | bytes 524288 | tf_op jit(solution)/shard_map/vmap()/gather | solution.py:49
  230.8 73.1 %while.12 = (s32[]{:T(128)}, f32[8,16,8,112]{3,2,1,0:T(8,128)S(1)}, f32[8,4096]{1,0:T(8,128)S(1)}, f32[32,24,128]{2,0,1:T(8,128)S(1)}, f32[32,24,128]{2,0,1:T(8,128)S(1)}, /*index=5*/s32[]{:T(128)}) while((s32[]{:T(128)}, f32[8,16,8,112]{3,2,1,0:T(8,128)S(1)}, f32[8,4096]{1,0:T(8,128)S(1)}, ...), condition=%wide.region_7.8_spmd.clone.clone, body=%wide.region_6.7_spmd.clone.clone.sunk | while | flops 234336256 | bytes 10379349 | solution.py:142
  234.4 0.6 fusion.548
  235.0 0.7 multiply_subtract_fusion.2
  244.2 0.7 multiply_subtract_fusion.2
  253.3 0.7 multiply_subtract_fusion.2
  262.4 0.7 multiply_subtract_fusion.2
  271.6 0.7 multiply_subtract_fusion.2
  280.7 0.7 multiply_subtract_fusion.2
  289.3 0.6 fusion.548
  289.8 0.7 multiply_subtract_fusion.2
  298.4 0.6 fusion.548
  299.0 0.7 multiply_subtract_fusion.2
  304.2 0.8 divide_log_fusion
  (221 shorter events, 70.0 us)
Async XLA Ops:
  0.0 7.4 %collective-permute-start = (f32[8,256]{1,0:T(8,128)}, f32[8,256]{1,0:T(8,128)S(1)}, u32[]{:S(2)}, u32[]{:S(2)}) collective-permute-start(f32[8,256]{1,0:T(8,128)} %param.9), channel_id=1, source_target_pairs={{0,1},{1,0},{2,3},{3,2},{4,5},{5,4},{6,7},{7,6},{8,9},{9,8},{10,11... | collective-permute-start | bytes 24584 | tf_op jit(solution)/shard_map/ppermute | solution.py:92
  1.3 16.0 %collective-permute-start.4 = (f32[8,8,112]{2,1,0:T(8,128)S(1)}, f32[8,8,112]{2,1,0:T(8,128)S(1)}, u32[]{:S(2)}, u32[]{:S(2)}) collective-permute-start(f32[8,8,112]{2,1,0:T(8,128)S(1)} %slice.34), channel_id=1, source_target_pairs={{0,1},{1,2},{2,3},{3,4},{4,5},{5,6},{6,7},{7,8},{8,9},{9,10},{10,1... | collective-permute-start | bytes 86024 | tf_op jit(solution)/shard_map/ppermute | solution.py:25
  3.3 14.0 %collective-permute-start.5 = (f32[8,8,112]{2,1,0:T(8,128)S(1)}, f32[8,8,112]{2,1,0:T(8,128)S(1)}, u32[]{:S(2)}, u32[]{:S(2)}) collective-permute-start(f32[8,8,112]{2,1,0:T(8,128)S(1)} %slice.36), channel_id=1, source_target_pairs={{1,0},{2,1},{3,2},{4,3},{5,4},{6,5},{7,6},{8,7},{9,8},{10,9},{11,1... | collective-permute-start | bytes 86024 | tf_op jit(solution)/shard_map/ppermute | solution.py:26
  7.0 0.7 copy-start.1
  7.0 5.5 %copy-start = (f32[16,896]{1,0:T(8,128)S(1)}, f32[16,896]{1,0:T(8,128)}, u32[]{:S(2)}) copy-start(f32[16,896]{1,0:T(8,128)} %param.8) | copy-start | bytes 172036
  7.1 5.6 %copy-start.2 = (s32[8]{0:T(128)S(1)}, s32[8]{0:T(128)}, u32[]{:S(2)}) copy-start(s32[8]{0:T(128)} %param.12) | copy-start | bytes 100
  7.7 6.5 %collective-permute-start.1 = (f32[8,512]{1,0:T(8,128)S(1)}, f32[8,512]{1,0:T(8,128)S(1)}, u32[]{:S(2)}, u32[]{:S(2)}) collective-permute-start(f32[8,512]{1,0:T(8,128)S(1)} %maximum_select_fusion.3), channel_id=1, source_target_pairs={{0,2},{1,3},{2,0},{3,1},{4,6},{5,7},{6,4},{7,5},{8,10},{9,11},{10,... | collective-permute-start | bytes 49160 | tf_op jit(solution)/shard_map/ppermute | solution.py:92
  14.3 9.6 %collective-permute-start.2 = (f32[8,1024]{1,0:T(8,128)S(1)}, f32[8,1024]{1,0:T(8,128)S(1)}, u32[]{:S(2)}, u32[]{:S(2)}) collective-permute-start(f32[8,1024]{1,0:T(8,128)S(1)} %maximum_select_fusion.2), channel_id=1, source_target_pairs={{0,4},{1,5},{2,6},{3,7},{4,0},{5,1},{6,2},{7,3},{8,12},{9,13},{10,... | collective-permute-start | bytes 98312 | tf_op jit(solution)/shard_map/ppermute | solution.py:92
  23.9 5.5 %collective-permute-start.3 = (f32[8,2048]{1,0:T(8,128)S(1)}, f32[8,2048]{1,0:T(8,128)S(1)}, u32[]{:S(2)}, u32[]{:S(2)}) collective-permute-start(f32[8,2048]{1,0:T(8,128)S(1)} %maximum_select_fusion.1), channel_id=1, source_target_pairs={{0,8},{1,9},{2,10},{3,11},{4,12},{5,13},{6,14},{7,15},{8,0},{9,1},... | collective-permute-start | bytes 196616 | tf_op jit(solution)/shard_map/ppermute | solution.py:92
